TPU v7x, 256 devices: a whole 4x4x8 slice. The times are simulated.
256 devices in a mesh: dp: 4 (over y), seq: 16 (over z, core), tensor: 4 (over x).
Axes of the slice: x: 4, y: 4, z: 8, core: 2. Of those that a mesh axis runs over, the one named last changes fastest.
Arguments:
- queries: bfloat16 [16384, 8192], P(('dp', 'seq'), 'tensor'), parts along dimension 0, may hold values from -110 to 110
- keys_values: bfloat16 [16384, 2, 1024], P(('dp', 'seq'), None, 'tensor'), parts along dimension 0, may hold values from -4.5 to 4.5
- out_weight: bfloat16 [8192, 8192], P('tensor', 'seq'), may hold values from -0.1875 to 0.1875
- residual: bfloat16 [16384, 8192], P(('dp', 'tensor'), 'seq'), parts along dimension 0, may hold values from -3 to 3
- segments: int32 [16384], P('dp'), parts along dimension 0, may hold values from 0 to 3, never falling along the last dimension, each value on 1 to 2048 neighbouring positions
Outputs:
- layer_out: bfloat16 [16384, 8192], P(('dp', 'tensor'), 'seq'), parts along dimension 0
There are 4 independent parts, one for each index of `dp`. A program takes and returns all parts, laid end to end along the dimension named above; an argument that names none is the same for every part. Nothing has to cross between parts.
Inputs may be any that keep to these rules, and one draw needn't show every extreme that they name: `segments`: segment numbers never fall along the tokens.
All inputs are finite; a program needn't handle non-finite values.
Results may differ from a plain program's by a relative error of at most 0.0085.
Values may be sent and summed in bfloat16 or wider, within the bound.
No kernel may reach another device: no remote copies, remote signals or barrier semaphores. Data moves between devices by JAX's collectives and lax.ppermute only.
A program may use at most 128 MiB of HBM per device.

v0:
```python
import jax
import jax.numpy as jnp
import numpy as np
from jax import lax
from jax.sharding import PartitionSpec as P

H = 64
KVH = 8
HD = 128
L = 4096
CHUNKS = 4


def attend_rows(query_head, key_head, value_head, doc_ids, first_row, rows):
    key_end = first_row + rows
    query_block = query_head[first_row:key_end]
    raw_scores = jnp.einsum(
        "qd,kd->qk", query_block, key_head[:key_end], preferred_element_type=jnp.float32
    ) * HD ** (-0.5)
    query_pos = first_row + jnp.arange(rows)[:, None]
    key_pos = jnp.arange(key_end)[None, :]
    same_doc = doc_ids[first_row:key_end, None] == doc_ids[None, :key_end]
    allowed = (key_pos <= query_pos) & same_doc
    masked = jnp.where(allowed, raw_scores, -1e30)
    highest = jnp.max(masked, axis=-1, keepdims=True)
    exponents = jnp.where(allowed, jnp.exp(masked - highest), 0.0)
    weights = (exponents / jnp.sum(exponents, axis=-1, keepdims=True)).astype(jnp.bfloat16)
    blended = jnp.einsum(
        "qk,kd->qd", weights, value_head[:key_end], preferred_element_type=jnp.float32
    )
    return blended.astype(jnp.bfloat16)


def on_device(queries, keys_values, out_weight, residual, segments):
    n_seq = lax.axis_size("seq")
    n_ten = lax.axis_size("tensor")
    seq_idx = lax.axis_index("seq")
    tok_dev = queries.shape[0]
    heads_ten = queries.shape[1] // HD
    heads_dev = heads_ten // n_seq
    assert heads_dev == 1
    group_size = H // KVH
    query_slab = queries.reshape(tok_dev, 1, heads_ten * HD)
    query_all = lax.all_to_all(query_slab, "seq", split_axis=2, concat_axis=0, tiled=True)
    query_head = query_all.reshape(query_all.shape[0], HD)
    rows_all = query_head.shape[0]
    assert rows_all == L
    pair_all = lax.all_gather(keys_values, "seq", axis=0, tiled=True)
    kv_local = seq_idx // group_size
    pair_head = lax.dynamic_slice_in_dim(pair_all, kv_local * HD, HD, axis=2)
    key_head = pair_head[:, 0, :]
    value_head = pair_head[:, 1, :]
    doc_ids = segments
    out_rows = rows_all // n_ten
    block_rows = out_rows // CHUNKS
    pieces = []
    for chunk in range(CHUNKS):
        blocks = [
            attend_rows(
                query_head,
                key_head,
                value_head,
                doc_ids,
                part * out_rows + chunk * block_rows,
                block_rows,
            )
            for part in range(n_ten)
        ]
        chunk_heads = jnp.concatenate(blocks, axis=0)
        gathered = lax.all_gather(chunk_heads, "seq", axis=1, tiled=True)
        projected = jnp.dot(gathered, out_weight, preferred_element_type=jnp.float32)
        pieces.append(lax.psum_scatter(projected, "tensor", scatter_dimension=0, tiled=True))
    summed = jnp.concatenate(pieces, axis=0)
    return (residual.astype(jnp.float32) + summed).astype(jnp.bfloat16)


def solution(mesh):
    placed = (
        P(("dp", "seq"), "tensor"),
        P(("dp", "seq"), None, "tensor"),
        P("tensor", "seq"),
        P(("dp", "tensor"), "seq"),
        P("dp"),
    )
    return jax.shard_map(
        on_device, mesh=mesh, in_specs=placed, out_specs=P(("dp", "tensor"), "seq"), check_vma=False
    )
```

profile of v0, /device:TPU:1, one launch (start us, length us, event | category | flops | bytes accessed | tf_op | source)
XLA Modules:
  0.0 436.0 jit_solution(1249033622516324133)
XLA Ops:
  8.4 5.9 %copy.44 = bf16[256,1,2048]{0,1,2:T(2,128)(2,1)} copy(bf16[256,1,2048]{2,0,1:T(8,128)(2,1)} %bitcast.316) | data formatting | bytes 2097152 | tf_op jit(solution)/shard_map/reshape | solution.py:43
  14.8 11.6 %reduce = bf16[2048,256]{1,0:T(8,128)(2,1)S(1)} reduce(bf16[2048,1,256]{2,1,0:T(2,128)(2,1)} %bitcast.306, bf16[]{:T(256)} %broadcast.172), dimensions={1}, to_apply=%bitcast.228.reduce_sub_computation | reduce | bytes 2097154
  27.6 10.0 %all-to-all-start = ((bf16[16,2,16384]{2,1,0:T(2,128)(2,1)}), bf16[16,2,16384]{2,1,0:T(2,128)(2,1)S(1)}, u32[]{:S(2)}, u32[]{:S(2)}) async-start(bf16[16,2,16384]{2,1,0:T(2,128)(2,1)} %reshape.191), calls=%async_computation | async-start | bytes 2097152 | tf_op jit(solution)/shard_map/all_to_all | solution.py:44
  38.3 34.3 %all-to-all-done = bf16[16,2,16384]{2,1,0:T(2,128)(2,1)S(1)} async-done(((bf16[16,2,16384]{2,1,0:T(2,128)(2,1)}), bf16[16,2,16384]{2,1,0:T(2,128)(2,1)S(1)}, u32[]{:S(2)}, u32[]{:S(2)}) %all-to-all-start) | async-done | bytes 1048608 | tf_op jit(solution)/shard_map/all_to_all | solution.py:44
  72.5 3.5 reshape.192
  77.8 3.2 fusion.130
  81.0 1.9 fusion.30
  87.6 2.3 fusion.65
  107.1 2.2 fusion.64
  121.4 2.0 fusion.63
  134.6 1.9 fusion.70
  137.3 4.7 %all-gather.14.cloned.1.call-done = bf16[1024,2048]{1,0:T(8,128)(2,1)} async-done(((bf16[1024,128]{1,0:T(8,128)(2,1)}), bf16[1024,2048]{1,0:T(8,128)(2,1)}) %all-gather.14.cloned.1.call-update) | async-done | bytes 4194320 | tf_op jit(solution)/shard_map/all_gather | solution.py:70
  142.0 5.9 %fusion.149 = f32[1024,512]{1,0:T(8,128)} fusion(bf16[1024,2048]{1,0:T(8,128)(2,1)} %all-gather.14.cloned.1.call-done, bf16[2048,512]{1,0:T(8,128)(2,1)S(1)} %copy-done), kind=kOutput, calls=%fused_computation.289 | convolution fusion | flops 2147483648 | bytes 8388608 | tf_op jit(solution)/shard_map/dot_general | solution.py:71
  147.9 43.5 %all-gather.12.cloned.1.call-done = bf16[1024,2048]{1,0:T(8,128)(2,1)} async-done(((bf16[1024,128]{1,0:T(8,128)(2,1)}), bf16[1024,2048]{1,0:T(8,128)(2,1)}) %all-gather.12.cloned.1.call-update) | async-done | bytes 4194320 | tf_op jit(solution)/shard_map/all_gather | solution.py:70
  191.5 5.9 %fusion.148 = f32[1024,512]{1,0:T(8,128)} fusion(bf16[1024,2048]{1,0:T(8,128)(2,1)} %all-gather.12.cloned.1.call-done, bf16[2048,512]{1,0:T(8,128)(2,1)S(1)} %copy-done), kind=kOutput, calls=%fused_computation.288 | convolution fusion | flops 2147483648 | bytes 8388608 | tf_op jit(solution)/shard_map/dot_general | solution.py:71
  197.7 43.0 %all-gather.10.cloned.1.call-done = bf16[1024,2048]{1,0:T(8,128)(2,1)} async-done(((bf16[1024,128]{1,0:T(8,128)(2,1)}), bf16[1024,2048]{1,0:T(8,128)(2,1)}) %all-gather.10.cloned.1.call-update) | async-done | bytes 4194320 | tf_op jit(solution)/shard_map/all_gather | solution.py:70
  240.7 5.8 %fusion.147 = f32[1024,512]{1,0:T(8,128)} fusion(bf16[1024,2048]{1,0:T(8,128)(2,1)} %all-gather.10.cloned.1.call-done, bf16[2048,512]{1,0:T(8,128)(2,1)S(1)} %copy-done), kind=kOutput, calls=%fused_computation.287 | convolution fusion | flops 2147483648 | bytes 8388608 | tf_op jit(solution)/shard_map/dot_general | solution.py:71
  246.6 43.3 %all-gather.8.cloned.1.call-done = bf16[1024,2048]{1,0:T(8,128)(2,1)} async-done(((bf16[1024,128]{1,0:T(8,128)(2,1)}), bf16[1024,2048]{1,0:T(8,128)(2,1)}) %all-gather.8.cloned.1.call-update) | async-done | bytes 4194320 | tf_op jit(solution)/shard_map/all_gather | solution.py:70
  289.9 5.8 %fusion.146 = f32[1024,512]{1,0:T(8,128)} fusion(bf16[1024,2048]{1,0:T(8,128)(2,1)} %all-gather.8.cloned.1.call-done, bf16[2048,512]{1,0:T(8,128)(2,1)S(1)} %copy-done), kind=kOutput, calls=%fused_computation.286 | convolution fusion | flops 2147483648 | bytes 8388608 | tf_op jit(solution)/shard_map/dot_general | solution.py:71
  295.8 26.6 %reduce-scatter.11.cloned.1.call-done = f32[256,512]{1,0:T(8,128)} async-done(((f32[1024,512]{1,0:T(8,128)}), f32[256,512]{1,0:T(8,128)}) %reduce-scatter.11.cloned.1.call-update) | async-done | bytes 524304 | tf_op jit(solution)/shard_map/reduce_scatter | solution.py:72
  322.4 34.6 %reduce-scatter.9.cloned.1.call-done = f32[256,512]{1,0:T(8,128)} async-done(((f32[1024,512]{1,0:T(8,128)}), f32[256,512]{1,0:T(8,128)}) %reduce-scatter.9.cloned.1.call-update) | async-done | bytes 524304 | tf_op jit(solution)/shard_map/reduce_scatter | solution.py:72
  357.0 34.6 %reduce-scatter.7.cloned.1.call-done = f32[256,512]{1,0:T(8,128)} async-done(((f32[1024,512]{1,0:T(8,128)}), f32[256,512]{1,0:T(8,128)}) %reduce-scatter.7.cloned.1.call-update) | async-done | bytes 524304 | tf_op jit(solution)/shard_map/reduce_scatter | solution.py:72
  391.6 34.6 %reduce-scatter.5.cloned.1.call-done = f32[256,512]{1,0:T(8,128)} async-done(((f32[1024,512]{1,0:T(8,128)}), f32[256,512]{1,0:T(8,128)}) %reduce-scatter.5.cloned.1.call-update) | async-done | bytes 524304 | tf_op jit(solution)/shard_map/reduce_scatter | solution.py:72
  426.2 2.8 fusion.36
  (109 shorter events, 52.0 us)
Async XLA Ops:
  6.5 135.5 %copy-start = (bf16[2048,512]{1,0:T(8,128)(2,1)S(1)}, bf16[2048,512]{1,0:T(8,128)(2,1)}, u32[]{:S(2)}) copy-start(bf16[2048,512]{1,0:T(8,128)(2,1)} %param.7) | copy-start | bytes 6291460
  6.5 71.3 %all-gather.6.cloned.1.call-start = ((), (), s32[]{:S(2)}) async-start(), calls=%async_computation.5 | async-start | bytes 4456448 | tf_op jit(solution)/shard_map/all_gather | solution.py:48
  26.5 11.7 %copy-start.1 = (s32[4096]{0:T(1024)S(1)}, s32[4096]{0:T(1024)}, u32[]{:S(2)}) copy-start(s32[4096]{0:T(1024)} %param.9) | copy-start | bytes 49156
  27.6 44.9 %all-to-all-start = ((bf16[16,2,16384]{2,1,0:T(2,128)(2,1)}), bf16[16,2,16384]{2,1,0:T(2,128)(2,1)S(1)}, u32[]{:S(2)}, u32[]{:S(2)}) async-start(bf16[16,2,16384]{2,1,0:T(2,128)(2,1)} %reshape.191), calls=%async_computation | async-start | bytes 2097152 | tf_op jit(solution)/shard_map/all_to_all | solution.py:44
  37.6 104.4 %all-gather.14.cloned.1.call-start = ((), (), s32[]{:S(2)}) async-start(), calls=%async_computation.12 | async-start | bytes 4456448 | tf_op jit(solution)/shard_map/all_gather | solution.py:70
  81.0 2.2 copy-start.3
  94.0 97.5 %all-gather.12.cloned.1.call-start = ((), (), s32[]{:S(2)}) async-start(), calls=%async_computation.10 | async-start | bytes 4456448 | tf_op jit(solution)/shard_map/all_gather | solution.py:70
  95.6 2.3 copy-start.4
  110.0 130.7 %all-gather.10.cloned.1.call-start = ((), (), s32[]{:S(2)}) async-start(), calls=%async_computation.8 | async-start | bytes 4456448 | tf_op jit(solution)/shard_map/all_gather | solution.py:70
  110.4 3.6 copy-start.5
  124.2 165.7 %all-gather.8.cloned.1.call-start = ((), (), s32[]{:S(2)}) async-start(), calls=%async_computation.6 | async-start | bytes 4456448 | tf_op jit(solution)/shard_map/all_gather | solution.py:70
  124.5 3.2 copy-start.6
  137.2 185.1 %reduce-scatter.11.cloned.1.call-start = ((), (), s32[]{:S(2)}) async-start(), calls=%async_computation.13 | async-start | bytes 2621440 | tf_op jit(solution)/shard_map/reduce_scatter | solution.py:72
  147.9 209.1 %reduce-scatter.9.cloned.1.call-start = ((), (), s32[]{:S(2)}) async-start(), calls=%async_computation.11 | async-start | bytes 2621440 | tf_op jit(solution)/shard_map/reduce_scatter | solution.py:72
  197.4 194.2 %reduce-scatter.7.cloned.1.call-start = ((), (), s32[]{:S(2)}) async-start(), calls=%async_computation.9 | async-start | bytes 2621440 | tf_op jit(solution)/shard_map/reduce_scatter | solution.py:72
  246.6 179.6 %copy-start.2 = (bf16[1024,512]{1,0:T(8,128)(2,1)S(1)}, bf16[1024,512]{1,0:T(8,128)(2,1)}, u32[]{:S(2)}) copy-start(bf16[1024,512]{1,0:T(8,128)(2,1)} %param.8) | copy-start | bytes 3145732
  246.6 179.6 %reduce-scatter.5.cloned.1.call-start = ((), (), s32[]{:S(2)}) async-start(), calls=%async_computation.7 | async-start | bytes 2621440 | tf_op jit(solution)/shard_map/reduce_scatter | solution.py:72
Sparse Core Ops, SparseCore 0:
  9.2 64.9 all-gather.5
  94.2 47.7 all-gather.13
  143.8 47.6 all-gather.11
  193.1 47.5 all-gather.9
  242.3 47.5 all-gather.7
  292.3 30.0 reduce-scatter.10
  324.9 31.9 reduce-scatter.8
  359.5 31.9 reduce-scatter.6
  394.1 32.0 reduce-scatter.4
where the time goes:
time: 440 us; the launch traced here: 436 us
  waiting for transfers between devices  299 us (68%)
  matrix products  62.2 us (14%)
  other arithmetic  33.2 us (8%)
  local copies, waits for them, and re-layouts  15.3 us (3%)
  between operations  14.2 us (3%)
  starting transfers between devices  11.8 us (3%)
    all_gather x4, waiting for transfers between devices, on_device(): gathered = lax.all_gather(chunk_heads, 'seq', axis=1, tiled=True)  135 us
    reduce_scatter x4, waiting for transfers between devices, on_device(): lax.psum_scatter(projected, 'tensor', scatter_dimension=0, tiled=True)  130 us
    all_to_all x1, waiting for transfers between devices, on_device(): lax.all_to_all(query_slab, 'seq', split_axis=2, concat_axis=0, tiled=True)  34.3 us
    dot_general x4, matrix products, on_device(): jnp.dot(gathered, out_weight, preferred_element_type=jnp.float32)  23.4 us
    dot_general x16, matrix products, attend_rows(): jnp.einsum('qk,kd->qd', weights, value_head[:key_end], preferred_element_...  21 us
    dot_general x16, matrix products, attend_rows(): jnp.einsum('qd,kd->qk', query_block, key_head[:key_end], preferred_elemen...  17.8 us
    reduce_sum x16, other arithmetic, attend_rows(): jnp.sum(exponents, axis=-1, keepdims=True)  15.8 us
    unnamed x1, other arithmetic  11.6 us
  transfers between devices with their start and end apart: 10, of which 9 were waited for; matrix products, arithmetic and copies ran while one was open for 21% of the time, Pallas kernels for 0%

commit v1 on v0

--- a/solution.py
+++ b/solution.py
@@ -67,7 +67,9 @@
             for part in range(n_ten)
         ]
         chunk_heads = jnp.concatenate(blocks, axis=0)
-        gathered = lax.all_gather(chunk_heads, "seq", axis=1, tiled=True)
+        gathered = jnp.concatenate(
+            lax.all_to_all(jnp.stack([chunk_heads] * lax.axis_size("seq")), "seq", 0, 0), axis=1
+        )
         projected = jnp.dot(gathered, out_weight, preferred_element_type=jnp.float32)
         pieces.append(lax.psum_scatter(projected, "tensor", scatter_dimension=0, tiled=True))
     summed = jnp.concatenate(pieces, axis=0)

time: 440 us -> 549 us (1.25)
  waiting for transfers between devices: 299 us -> 372 us
  starting transfers between devices: 11.8 us -> 33.1 us
  local copies, waits for them, and re-layouts: 15.3 us -> 29.1 us
    all_to_all x0 -> x4, waiting for transfers between devices: none -> 306 us  [on_device(): lax.all_to_all(jnp.stack([chunk_heads] * lax.axis_size('seq')), 'seq', 0, 0)]
    all_gather x4 -> x0, waiting for transfers between devices: 135 us -> none  [on_device(): gathered = lax.all_gather(chunk_heads, 'seq', axis=1, tiled=True)]
    reduce_scatter x4, waiting for transfers between devices: 130 us -> 31.6 us  [on_device(): lax.psum_scatter(projected, 'tensor', scatter_dimension=0, tiled=True)]
    all_to_all x0 -> x4, starting transfers between devices: none -> 22 us  [on_device(): lax.all_to_all(jnp.stack([chunk_heads] * lax.axis_size('seq')), 'seq', 0, 0)]
    another operation x0 -> x4, local copies, waits for them, and re-layouts: none -> 9.96 us  [on_device(): jnp.stack([chunk_heads] * lax.axis_size('seq'))]
  transfers between devices with their start and end apart: 10 -> 10, of which waited for: 9 -> 6; matrix products, arithmetic and copies ran while one was open for 21% -> 18% of each run, Pallas kernels for 0% -> 0%
where the time goes in v1:
time: 549 us; the launch traced here: 546 us
  waiting for transfers between devices  372 us (68%)
  matrix products  65.2 us (12%)
  starting transfers between devices  33.1 us (6%)
  other arithmetic  32.5 us (6%)
  local copies, waits for them, and re-layouts  29.1 us (5%)
  between operations  13.9 us (3%)
    all_to_all x4, waiting for transfers between devices, on_device(): lax.all_to_all(jnp.stack([chunk_heads] * lax.axis_size('seq')), 'seq', 0, 0)  306 us
    all_to_all x1, waiting for transfers between devices, on_device(): lax.all_to_all(query_slab, 'seq', split_axis=2, concat_axis=0, tiled=True)  34.2 us
    reduce_scatter x4, waiting for transfers between devices, on_device(): lax.psum_scatter(projected, 'tensor', scatter_dimension=0, tiled=True)  31.6 us
    dot_general x4, matrix products, on_device(): jnp.dot(gathered, out_weight, preferred_element_type=jnp.float32)  23.6 us
    all_to_all x4, starting transfers between devices, on_device(): lax.all_to_all(jnp.stack([chunk_heads] * lax.axis_size('seq')), 'seq', 0, 0)  22 us
    dot_general x16, matrix products, attend_rows(): jnp.einsum('qk,kd->qd', weights, value_head[:key_end], preferred_element_...  21.3 us
    dot_general x16, matrix products, attend_rows(): jnp.einsum('qd,kd->qk', query_block, key_head[:key_end], preferred_elemen...  20.3 us
    reduce_sum x16, other arithmetic, attend_rows(): jnp.sum(exponents, axis=-1, keepdims=True)  15.8 us
  transfers between devices with their start and end apart: 10, of which 6 were waited for; matrix products, arithmetic and copies ran while one was open for 18% of the time, Pallas kernels for 0%

profile of v1, /device:TPU:1, one launch (start us, length us, event | category | flops | bytes accessed | tf_op | source)
XLA Modules:
  0.0 545.5 jit_solution(14238716878264238421)
XLA Ops:
  8.4 5.9 %copy.56 = bf16[256,1,2048]{0,1,2:T(2,128)(2,1)} copy(bf16[256,1,2048]{2,0,1:T(8,128)(2,1)} %bitcast.328) | data formatting | bytes 2097152 | tf_op jit(solution)/shard_map/reshape | solution.py:43
  14.8 11.6 %reduce = bf16[2048,256]{1,0:T(8,128)(2,1)S(1)} reduce(bf16[2048,1,256]{2,1,0:T(2,128)(2,1)} %bitcast.318, bf16[]{:T(256)} %broadcast.180), dimensions={1}, to_apply=%bitcast.240.reduce_sub_computation | reduce | bytes 2097154
  27.6 10.6 %all-to-all-start = ((bf16[16,2,16384]{2,1,0:T(2,128)(2,1)}), bf16[16,2,16384]{2,1,0:T(2,128)(2,1)S(1)}, u32[]{:S(2)}, u32[]{:S(2)}) async-start(bf16[16,2,16384]{2,1,0:T(2,128)(2,1)} %reshape.231), calls=%async_computation | async-start | bytes 2097152 | tf_op jit(solution)/shard_map/all_to_all | solution.py:44
  38.3 34.2 %all-to-all-done = bf16[16,2,16384]{2,1,0:T(2,128)(2,1)S(1)} async-done(((bf16[16,2,16384]{2,1,0:T(2,128)(2,1)}), bf16[16,2,16384]{2,1,0:T(2,128)(2,1)S(1)}, u32[]{:S(2)}, u32[]{:S(2)}) %all-to-all-start) | async-done | bytes 1048608 | tf_op jit(solution)/shard_map/all_to_all | solution.py:44
  72.5 3.5 reshape.232
  92.7 2.5 stack.9
  95.2 4.9 all-to-all-start.2
  113.9 79.6 %all-to-all-done.2 = bf16[16,1024,128]{1,2,0:T(8,128)(2,1)} async-done(((bf16[16,1024,128]{1,2,0:T(8,128)(2,1)}), bf16[16,1024,128]{1,2,0:T(8,128)(2,1)}, u32[]{:S(2)}, u32[]{:S(2)}) %all-to-all-start.2) | async-done | bytes 4194336 | tf_op jit(solution)/shard_map/all_to_all | solution.py:71
  193.5 2.5 stack.8
  196.0 5.9 %all-to-all-start.1 = ((bf16[16,1024,128]{1,2,0:T(8,128)(2,1)}), bf16[16,1024,128]{1,2,0:T(8,128)(2,1)}, u32[]{:S(2)}, u32[]{:S(2)}) async-start(bf16[16,1024,128]{1,2,0:T(8,128)(2,1)} %stack.8), calls=%async_computation.1 | async-start | bytes 8388608 | tf_op jit(solution)/shard_map/all_to_all | solution.py:71
  219.4 75.9 %all-to-all-done.1 = bf16[16,1024,128]{1,2,0:T(8,128)(2,1)} async-done(((bf16[16,1024,128]{1,2,0:T(8,128)(2,1)}), bf16[16,1024,128]{1,2,0:T(8,128)(2,1)}, u32[]{:S(2)}, u32[]{:S(2)}) %all-to-all-start.1) | async-done | bytes 4194336 | tf_op jit(solution)/shard_map/all_to_all | solution.py:71
  295.2 2.5 stack.11
  297.7 5.5 %all-to-all-start.4 = ((bf16[16,1024,128]{1,2,0:T(8,128)(2,1)}), bf16[16,1024,128]{1,2,0:T(8,128)(2,1)}, u32[]{:S(2)}, u32[]{:S(2)}) async-start(bf16[16,1024,128]{1,2,0:T(8,128)(2,1)} %stack.11), calls=%async_computation.7 | async-start | bytes 8388608 | tf_op jit(solution)/shard_map/all_to_all | solution.py:71
  306.1 2.8 fusion.136
  308.9 5.9 %fusion.147 = f32[1024,512]{1,0:T(8,128)} fusion(bf16[1024,2048]{0,1:T(8,128)(2,1)} %bitcast.37, bf16[2048,512]{1,0:T(8,128)(2,1)S(1)} %copy-done), kind=kOutput, calls=%fused_computation.287 | convolution fusion | flops 2147483648 | bytes 8388608 | tf_op jit(solution)/shard_map/dot_general | solution.py:73
  327.9 68.8 %all-to-all-done.4 = bf16[16,1024,128]{1,2,0:T(8,128)(2,1)} async-done(((bf16[16,1024,128]{1,2,0:T(8,128)(2,1)}), bf16[16,1024,128]{1,2,0:T(8,128)(2,1)}, u32[]{:S(2)}, u32[]{:S(2)}) %all-to-all-start.4) | async-done | bytes 4194336 | tf_op jit(solution)/shard_map/all_to_all | solution.py:71
  396.7 2.5 stack.10
  399.2 5.7 %all-to-all-start.3 = ((bf16[16,1024,128]{1,2,0:T(8,128)(2,1)}), bf16[16,1024,128]{1,2,0:T(8,128)(2,1)}, u32[]{:S(2)}, u32[]{:S(2)}) async-start(bf16[16,1024,128]{1,2,0:T(8,128)(2,1)} %stack.10), calls=%async_computation.5 | async-start | bytes 8388608 | tf_op jit(solution)/shard_map/all_to_all | solution.py:71
  404.9 5.9 %fusion.146 = f32[1024,512]{1,0:T(8,128)} fusion(bf16[1024,2048]{0,1:T(8,128)(2,1)} %bitcast.19, bf16[2048,512]{1,0:T(8,128)(2,1)S(1)} %copy-done), kind=kOutput, calls=%fused_computation.286 | convolution fusion | flops 2147483648 | bytes 8388608 | tf_op jit(solution)/shard_map/dot_general | solution.py:73
  410.9 5.9 %fusion.149 = f32[1024,512]{1,0:T(8,128)} fusion(bf16[1024,2048]{0,1:T(8,128)(2,1)} %bitcast.73, bf16[2048,512]{1,0:T(8,128)(2,1)S(1)} %copy-done), kind=kOutput, calls=%fused_computation.289 | convolution fusion | flops 2147483648 | bytes 8388608 | tf_op jit(solution)/shard_map/dot_general | solution.py:73
  416.8 81.6 %all-to-all-done.3 = bf16[16,1024,128]{1,2,0:T(8,128)(2,1)} async-done(((bf16[16,1024,128]{1,2,0:T(8,128)(2,1)}), bf16[16,1024,128]{1,2,0:T(8,128)(2,1)}, u32[]{:S(2)}, u32[]{:S(2)}) %all-to-all-start.3) | async-done | bytes 4194336 | tf_op jit(solution)/shard_map/all_to_all | solution.py:71
  498.4 6.0 %fusion.148 = f32[1024,512]{1,0:T(8,128)} fusion(bf16[1024,2048]{0,1:T(8,128)(2,1)} %bitcast.55, bf16[2048,512]{1,0:T(8,128)(2,1)S(1)} %copy-done), kind=kOutput, calls=%fused_computation.288 | convolution fusion | flops 2147483648 | bytes 8388608 | tf_op jit(solution)/shard_map/dot_general | solution.py:73
  504.5 31.5 %reduce-scatter.9.cloned.1.call-done = f32[256,512]{1,0:T(8,128)} async-done(((f32[1024,512]{1,0:T(8,128)}), f32[256,512]{1,0:T(8,128)}) %reduce-scatter.9.cloned.1.call-update) | async-done | bytes 524304 | tf_op jit(solution)/shard_map/reduce_scatter | solution.py:74
  536.0 2.8 fusion.36
  (117 shorter events, 67.2 us)
Async XLA Ops:
  6.5 302.4 %copy-start = (bf16[2048,512]{1,0:T(8,128)(2,1)S(1)}, bf16[2048,512]{1,0:T(8,128)(2,1)}, u32[]{:S(2)}) copy-start(bf16[2048,512]{1,0:T(8,128)(2,1)} %param.7) | copy-start | bytes 6291460
  6.5 71.3 %all-gather.2.cloned.1.call-start = ((), (), s32[]{:S(2)}) async-start(), calls=%async_computation.9 | async-start | bytes 4456448 | tf_op jit(solution)/shard_map/all_gather | solution.py:48
  26.5 11.7 %copy-start.1 = (s32[4096]{0:T(1024)S(1)}, s32[4096]{0:T(1024)}, u32[]{:S(2)}) copy-start(s32[4096]{0:T(1024)} %param.9) | copy-start | bytes 49156
  27.6 44.9 %all-to-all-start = ((bf16[16,2,16384]{2,1,0:T(2,128)(2,1)}), bf16[16,2,16384]{2,1,0:T(2,128)(2,1)S(1)}, u32[]{:S(2)}, u32[]{:S(2)}) async-start(bf16[16,2,16384]{2,1,0:T(2,128)(2,1)} %reshape.231), calls=%async_computation | async-start | bytes 2097152 | tf_op jit(solution)/shard_map/all_to_all | solution.py:44
  77.8 3.6 copy-start.5
  95.2 98.3 %all-to-all-start.2 = ((bf16[16,1024,128]{1,2,0:T(8,128)(2,1)}), bf16[16,1024,128]{1,2,0:T(8,128)(2,1)}, u32[]{:S(2)}, u32[]{:S(2)}) async-start(bf16[16,1024,128]{1,2,0:T(8,128)(2,1)} %stack.9), calls=%async_computation.3 | async-start | bytes 8388608 | tf_op jit(solution)/shard_map/all_to_all | solution.py:71
  100.1 3.3 copy-start.6
  196.0 99.2 %all-to-all-start.1 = ((bf16[16,1024,128]{1,2,0:T(8,128)(2,1)}), bf16[16,1024,128]{1,2,0:T(8,128)(2,1)}, u32[]{:S(2)}, u32[]{:S(2)}) async-start(bf16[16,1024,128]{1,2,0:T(8,128)(2,1)} %stack.8), calls=%async_computation.1 | async-start | bytes 8388608 | tf_op jit(solution)/shard_map/all_to_all | solution.py:71
  203.6 2.6 copy-start.7
  297.7 99.0 %all-to-all-start.4 = ((bf16[16,1024,128]{1,2,0:T(8,128)(2,1)}), bf16[16,1024,128]{1,2,0:T(8,128)(2,1)}, u32[]{:S(2)}, u32[]{:S(2)}) async-start(bf16[16,1024,128]{1,2,0:T(8,128)(2,1)} %stack.11), calls=%async_computation.7 | async-start | bytes 8388608 | tf_op jit(solution)/shard_map/all_to_all | solution.py:71
  303.2 201.2 %reduce-scatter.7.cloned.1.call-start = ((), (), s32[]{:S(2)}) async-start(), calls=%async_computation.11 | async-start | bytes 2621440 | tf_op jit(solution)/shard_map/reduce_scatter | solution.py:74
  305.0 0.9 copy-start.4
  314.9 1.9 copy-start.2
  314.9 3.0 copy-start.8
  399.2 99.2 %all-to-all-start.3 = ((bf16[16,1024,128]{1,2,0:T(8,128)(2,1)}), bf16[16,1024,128]{1,2,0:T(8,128)(2,1)}, u32[]{:S(2)}, u32[]{:S(2)}) async-start(bf16[16,1024,128]{1,2,0:T(8,128)(2,1)} %stack.10), calls=%async_computation.5 | async-start | bytes 8388608 | tf_op jit(solution)/shard_map/all_to_all | solution.py:71
  404.9 99.6 %reduce-scatter.5.cloned.1.call-start = ((), (), s32[]{:S(2)}) async-start(), calls=%async_computation.10 | async-start | bytes 2621440 | tf_op jit(solution)/shard_map/reduce_scatter | solution.py:74
  410.8 93.6 %reduce-scatter.11.cloned.1.call-start = ((), (), s32[]{:S(2)}) async-start(), calls=%async_computation.13 | async-start | bytes 2621440 | tf_op jit(solution)/shard_map/reduce_scatter | solution.py:74
  416.8 119.2 %reduce-scatter.9.cloned.1.call-start = ((), (), s32[]{:S(2)}) async-start(), calls=%async_computation.12 | async-start | bytes 2621440 | tf_op jit(solution)/shard_map/reduce_scatter | solution.py:74
  498.4 37.6 %copy-start.3 = (bf16[1024,512]{1,0:T(8,128)(2,1)S(1)}, bf16[1024,512]{1,0:T(8,128)(2,1)}, u32[]{:S(2)}) copy-start(bf16[1024,512]{1,0:T(8,128)(2,1)} %param.8) | copy-start | bytes 3145732
Sparse Core Ops, SparseCore 0:
  9.2 64.9 all-gather.1
  315.0 33.1 reduce-scatter.6
  411.0 33.1 reduce-scatter.4
  446.6 32.0 reduce-scatter.10
  504.5 31.4 reduce-scatter.8
